TPU v7x, 128 devices: a whole 4x4x4 slice. The times are simulated.
128 devices in a mesh: ctx: 32 (over x, y, core), head: 4 (over z).
Axes of the slice: x: 4, y: 4, z: 4, core: 2. Of those that a mesh axis runs over, the one named last changes fastest.
Arguments:
- x_in: bfloat16 [16384, 1, 8192], P('ctx', None, 'head'), may hold values from -6 to 6
- z_in: bfloat16 [16384, 1, 8192], P('ctx', None, 'head')
- bc_in: bfloat16 [16384, 1, 256], P('ctx'), may hold values from -6 to 6
- dt_in: float32 [16384, 1, 128], P('ctx', None, 'head'), may hold values from -3 to 3
- dt_bias: float32 [128], P('head')
- a_log: float32 [128], P('head'), may hold values from -1.5 to 0.5
- skip: float32 [128], P('head'), may hold values from 0.5 to 1.5
- conv_x: bfloat16 [4, 8192], P(None, 'head'), may hold values from -3 to 3
- conv_bc: bfloat16 [4, 256], replicated, may hold values from -3 to 3
- norm_gain: float32 [8192], P('head'), may hold values from 0.1 to 1.9
- w_out: bfloat16 [8192, 4096], P('head'), may hold values from -0.0625 to 0.0625
- requests: int32 [256], P('ctx'), may hold values from 0 to 1, as said below
- step_x: bfloat16 [4, 256, 8192], P(None, 'ctx', 'head'), may hold values from -6 to 6
- step_z: bfloat16 [4, 256, 8192], P(None, 'ctx', 'head'), may hold values from -6 to 6
- step_bc: bfloat16 [4, 256, 256], P(None, 'ctx'), may hold values from -6 to 6
- step_dt: float32 [4, 256, 128], P(None, 'ctx', 'head'), may hold values from -3 to 3
Outputs:
- out: bfloat16 [16384, 1, 4096], P(('ctx', 'head'))
- dec_out: bfloat16 [4, 256, 8192], P(None, 'ctx', 'head')
Inputs may be any that keep to these rules, and one draw needn't show every extreme that they name: Slot r is decoded on index r // 8 of ctx. Each index's 8 slots hold its requests first, then empty slots marked 1; every index has one request or more, and some index has all 8 slots in use.
All inputs are finite; a program needn't handle non-finite values.
Results may differ from a plain program's by a relative error of at most 0.007.
Values may be sent and summed in bfloat16 or wider, within the bound.
No kernel may reach another device: no remote copies, remote signals or barrier semaphores. Data moves between devices by JAX's collectives and lax.ppermute only.
A program may use at most 256 MiB of HBM per device.

v0:
```python
import jax
import jax.numpy as jnp
from jax import lax
from jax.sharding import PartitionSpec as P

norm_eps = 1e-05


def passed_along(value, axis, steps):
    count = lax.axis_size(axis)
    leading, last = (max(0, -steps), min(count, count - steps))
    return lax.ppermute(value, axis, [(source, source + steps) for source in range(leading, last)])


def prefix(value, axis, combine, identity):
    count, here = (lax.axis_size(axis), lax.axis_index(axis))
    everything = jax.tree.map(lambda part: lax.all_gather(part, axis), value)
    start = jax.tree.map(
        lambda part, zero: jnp.broadcast_to(jnp.asarray(zero, part.dtype), part.shape),
        value,
        identity,
    )

    def step(k, before):
        reached = k < here
        new = combine(before, jax.tree.map(lambda part: part[k], everything))
        return jax.tree.map(lambda a, b: jnp.where(reached, a, b), new, before)

    return lax.fori_loop(0, count, step, start)


def spread(value, axis, root):
    mine = lax.axis_index(axis) == root
    return lax.psum(jnp.where(mine, value, jnp.zeros_like(value)), axis)


def conv_silu(window, weight, length):
    running_sum = jnp.zeros((length,) + window.shape[1:], jnp.float32)
    for offset in range(weight.shape[0]):
        running_sum = running_sum + window[offset : offset + length].astype(jnp.float32) * weight[
            offset
        ].astype(jnp.float32)
    return jax.nn.silu(running_sum).astype(jnp.bfloat16)


def chain_pair(earlier_pair, later_pair):
    return (
        earlier_pair[0] * later_pair[0],
        later_pair[0][..., None, None] * earlier_pair[1] + later_pair[1],
    )


def body(
    x_in,
    z_in,
    bc_in,
    dt_in,
    dt_bias,
    a_log,
    skip,
    conv_x,
    conv_bc,
    norm_gain,
    w_out,
    requests,
    step_x,
    step_z,
    step_bc,
    step_dt,
):
    block_len, prompts, inner_loc = x_in.shape
    heads_loc = dt_in.shape[2]
    head_dim = inner_loc // heads_loc
    state_dim = bc_in.shape[2] // 2
    conv_taps = conv_x.shape[0]
    edge_x, edge_bc = passed_along(
        (x_in[block_len - conv_taps + 1 :], bc_in[block_len - conv_taps + 1 :]), "ctx", 1
    )
    x_conv = conv_silu(jnp.concatenate([edge_x, x_in], axis=0), conv_x, block_len)
    bc_conv = conv_silu(jnp.concatenate([edge_bc, bc_in], axis=0), conv_bc, block_len)
    b_rows = bc_conv[..., :state_dim]
    c_rows = bc_conv[..., state_dim:]
    decay_rates = -jnp.exp(a_log)
    dt_full = jax.nn.softplus(dt_in + dt_bias)
    cum_log = jnp.cumsum(dt_full * decay_rates, axis=0)
    cum_heads = jnp.transpose(cum_log, (1, 2, 0))
    dt_heads = jnp.transpose(dt_full, (1, 2, 0))
    x_heads = x_conv.reshape(block_len, prompts, heads_loc, head_dim)
    scores = jnp.einsum("ipn,jpn->pij", c_rows, b_rows, preferred_element_type=jnp.float32)
    position = lax.iota(jnp.int32, block_len)
    causal = position[:, None] >= position[None, :]
    gaps = jnp.where(causal, cum_heads[..., :, None] - cum_heads[..., None, :], -jnp.inf)
    mixing = (scores[:, None] * jnp.exp(gaps) * dt_heads[..., None, :]).astype(jnp.bfloat16)
    y_intra = jnp.einsum("phij,jphd->iphd", mixing, x_heads, preferred_element_type=jnp.float32)
    block_log = cum_heads[..., -1]
    tail_weights = jnp.transpose(jnp.exp(block_log[..., None] - cum_heads) * dt_heads, (2, 0, 1))
    weighted_x = (x_heads * tail_weights[..., None]).astype(jnp.bfloat16)
    s_local = jnp.einsum("jphd,jpn->phdn", weighted_x, b_rows, preferred_element_type=jnp.float32)
    block_decay = jnp.exp(block_log)
    identity_pair = (jnp.ones_like(block_decay), jnp.zeros_like(s_local))
    decay_before, s_before = prefix((block_decay, s_local), "ctx", chain_pair, identity_pair)
    y_inter = (
        jnp.einsum(
            "ipn,phdn->iphd", c_rows.astype(jnp.float32), s_before, precision=lax.Precision.HIGHEST
        )
        * jnp.exp(cum_log)[..., None]
    )
    y_all = y_intra + y_inter + skip[:, None] * x_heads.astype(jnp.float32)
    gated_out = y_all.reshape(block_len, prompts, inner_loc) * jax.nn.silu(z_in.astype(jnp.float32))
    square_sums = lax.psum(jnp.sum(gated_out * gated_out, axis=-1), "head")
    inner_total = inner_loc * lax.axis_size("head")
    normed = (
        gated_out * lax.rsqrt(square_sums / inner_total + norm_eps)[..., None] * norm_gain
    ).astype(jnp.bfloat16)
    projected = lax.psum_scatter(
        jnp.einsum("tpi,id->tpd", normed, w_out, preferred_element_type=jnp.float32),
        "head",
        scatter_dimension=0,
        tiled=True,
    )
    out = projected.astype(jnp.bfloat16)
    tail_x = x_in[block_len - conv_taps + 1 :].astype(jnp.float32)
    tail_bc = bc_in[block_len - conv_taps + 1 :].astype(jnp.float32)
    s_after = block_decay[..., None, None] * s_before + s_local
    final_state, final_x, final_bc = (
        spread(s_after, "ctx", lax.axis_size("ctx") - 1),
        spread(tail_x, "ctx", lax.axis_size("ctx") - 1),
        spread(tail_bc, "ctx", lax.axis_size("ctx") - 1),
    )
    slot_count = requests.shape[0]
    slot_pick = (requests[:, None] == lax.iota(jnp.int32, prompts)[None, :]).astype(jnp.float32)
    live_slots = requests < prompts
    states = jnp.einsum("rp,phdn->rhdn", slot_pick, final_state, precision=lax.Precision.HIGHEST)
    hist_x = jnp.einsum("rp,kpi->kri", slot_pick, final_x, precision=lax.Precision.HIGHEST).astype(
        jnp.bfloat16
    )
    hist_bc = jnp.einsum(
        "rp,kpi->kri", slot_pick, final_bc, precision=lax.Precision.HIGHEST
    ).astype(jnp.bfloat16)
    outputs = []
    for step_index in range(step_x.shape[0]):
        window_x = jnp.concatenate([hist_x, step_x[step_index][None]], axis=0)
        window_bc = jnp.concatenate([hist_bc, step_bc[step_index][None]], axis=0)
        new_x = conv_silu(window_x, conv_x, 1)[0]
        new_bc = conv_silu(window_bc, conv_bc, 1)[0]
        hist_x = window_x[1:]
        hist_bc = window_bc[1:]
        dt_step = jax.nn.softplus(step_dt[step_index] + dt_bias)
        x_step = new_x.reshape(slot_count, heads_loc, head_dim).astype(jnp.float32)
        b_step = new_bc[:, :state_dim].astype(jnp.float32)
        c_step = new_bc[:, state_dim:].astype(jnp.float32)
        states = (
            jnp.exp(dt_step * decay_rates)[..., None, None] * states
            + (dt_step[..., None] * x_step)[..., None] * b_step[:, None, None, :]
        )
        y_step = (
            jnp.einsum("rn,rhdn->rhd", c_step, states, precision=lax.Precision.HIGHEST)
            + skip[:, None] * x_step
        )
        gated_step = y_step.reshape(slot_count, inner_loc) * jax.nn.silu(
            step_z[step_index].astype(jnp.float32)
        )
        outputs.append(jnp.where(live_slots[:, None], gated_step, 0.0).astype(jnp.bfloat16))
    return (out, jnp.stack(outputs))


def solution(mesh):
    placed = (
        P("ctx", None, "head"),
        P("ctx", None, "head"),
        P("ctx", None, None),
        P("ctx", None, "head"),
        P("head"),
        P("head"),
        P("head"),
        P(None, "head"),
        P(),
        P("head"),
        P("head", None),
        P("ctx"),
        P(None, "ctx", "head"),
        P(None, "ctx", "head"),
        P(None, "ctx", None),
        P(None, "ctx", "head"),
    )
    return jax.shard_map(
        body,
        mesh=mesh,
        in_specs=placed,
        out_specs=(P(("ctx", "head"), None, None), P(None, "ctx", "head")),
        check_vma=False,
    )
```

profile of v0, /device:TPU:0, one launch (start us, length us, event | category | flops | bytes accessed | tf_op | source)
XLA Modules:
  0.0 493.6 jit_solution(4286240662727842826)
XLA Ops:
  8.3 2.1 collective-permute-start
  11.1 3.5 collective-permute-start.1
  20.8 2.9 copy.73
  23.7 1.7 multiply_convert_fusion.6
  25.9 7.3 %fusion.16 = (bf16[512,1,2048]{0,2,1:T(8,128)(2,1)S(1)}, bf16[512,1,2048]{0,2,1:T(8,128)(2,1)}) fusion(f32[2048]{0:T(1024)S(1)} %bitcast.190, bf16[512,1,2048]{0,2,1:T(8,128)(2,1)S(1)} %copy.73, f32[2048]{0:T(1024)S(1)} %bitcast.193, bf16[3,1,2048]{0,2,1:T(8,128)(2,1)} %collective-permute-done, f32[2048]{0:T(1024)S(1)} %bitcast.187, f32[2048]{0:T(1024)S(1)} %bitcast.184, ...), kind=kLoop, calls=%fused_computation.27 | loop fusion | flops 29360128 | bytes 10530816 | tf_op jit(solution)/shard_map/convert_element_type | solution.py:97
  33.3 1.7 fusion.68
  36.5 3.9 copy.84
  40.4 24.0 %all-gather = f32[32,32,1]{1,2,0:T(1,128)} all-gather(f32[1,32,1]{1,2,0:T(1,128)S(1)} %copy.80), channel_id=2, replica_groups=mesh['ctx'=32,'head'=4] {'ctx'}, dimensions={0}, use_global_device_ids=true | all-gather | bytes 4224 | tf_op jit(solution)/shard_map/all_gather | solution.py:17
  66.1 84.6 %all-gather.4.cloned.1.call-done = f32[1024,64,128]{2,1,0:T(8,128)} async-done(((f32[32,64,128]{2,1,0:T(8,128)}), f32[1024,64,128]{2,1,0:T(8,128)}) %all-gather.4.cloned.1.call-update) | async-done | bytes 33554448 | tf_op jit(solution)/shard_map/all_gather | solution.py:17
  150.7 86.4 %while.14 = (s32[]{:T(128)}, f32[1,32,64,128]{3,2,1,0:T(8,128)S(1)}, s32[]{:T(128)}, f32[32,1,32]{2,1,0:T(1,128)}, f32[32,1,32,64,128]{4,3,2,1,0:T(8,128)}, /*index=5*/s32[]{:T(128)}, s32[]{:T(128)}) while((s32[]{:T(128)}, f32[1,32,64,128]{3,2,1,0:T(8,128)S(1)}, s32[]{:T(128)}, f32[32,1,32]{2,1,0:T(1,128)}, ...), condition=%wide.region_3.4_spmd.clone, body=%wide.region_2.3_spmd.clone.sunk | while | flops 1048580 | bytes 3146217 | solution.py:29
  152.0 1.5 fusion.147
  154.7 1.5 fusion.147
  157.3 1.5 fusion.147
  160.0 1.5 fusion.147
  162.7 1.5 fusion.147
  165.4 1.5 fusion.147
  168.1 1.5 fusion.147
  170.9 1.5 fusion.147
  173.5 1.5 fusion.147
  176.2 1.5 fusion.147
  178.8 1.5 fusion.147
  181.5 1.5 fusion.147
  184.2 1.5 fusion.147
  187.0 1.5 fusion.147
  195.1 1.5 fusion.147
  200.5 1.5 fusion.147
  203.3 1.5 fusion.147
  205.9 1.5 fusion.147
  208.6 1.5 fusion.147
  214.0 1.5 fusion.147
  219.5 1.5 fusion.147
  222.2 1.5 fusion.147
  224.9 1.5 fusion.147
  227.6 1.5 fusion.147
  230.3 1.5 fusion.147
  235.6 1.5 fusion.147
  237.1 3.8 fusion.63
  240.9 1.8 fusion.62
  242.8 13.2 %fusion.15 = f32[512,1,32,64]{0,3,2,1:T(8,128)S(1)} fusion(f32[32,64,512]{2,1,0:T(8,128)} %fusion.63, bf16[512,32,64]{0,2,1:T(8,128)(2,1)} %bitcast.171, f32[32,512]{1,0:T(8,128)S(1)} %get-tuple-element.173, f32[32,512]{1,0:T(8,128)} %bitcast_add_fusion.2, f32[512,512]{1,0:T(8,128)S(1)} %fusion.70, pred[512,512]{1,0:T(8,128)(4,1)} %iota_compare_fusion, ...), kind=kOutput, calls=%fused_computation.25 | convolution fusion | flops 1120927744 | bytes 14090368 | tf_op jit(solution)/shard_map/phij,jphd->iphd/dot_general | solution.py:94
  256.0 3.4 multiply_reduce_fusion
  259.4 10.8 %psum.28 = f32[512,1]{0,1:T(1,128)S(1)} all-reduce(f32[512,1]{0,1:T(1,128)S(1)} %bitcast.211), channel_id=1, replica_groups=mesh['ctx'=32,'head'=4] {'head'}, use_global_device_ids=true, to_apply=%region_5.6 | all-reduce | flops 512 | bytes 4096 | tf_op jit(solution)/shard_map/psum | solution.py:110
  270.2 16.1 %convolution_bitcast_fusion = f32[512,1,4096]{2,0,1:T(8,128)} fusion(bf16[2048,4096]{1,0:T(8,128)(2,1)} %param.28, f32[512,1,2048]{0,2,1:T(8,128)} %get-tuple-element.161, f32[2048]{0:T(1024)S(1)} %copy-done.11, f32[512]{0:T(512)S(1)} %bitcast.212), kind=kOutput, calls=%fused_computation.16 | convolution fusion | flops 8593080320 | bytes 29370368 | tf_op jit(solution)/shard_map/tpi,id->tpd/dot_general | solution.py:116
  287.5 136.8 %all-reduce = (f32[3,256]{1,0:T(4,128)S(1)}, f32[3,2048]{0,1:T(8,128)S(1)}) all-reduce(f32[3,256]{1,0:T(4,128)S(1)} %select_bitcast_fusion.1, f32[3,2048]{0,1:T(8,128)S(1)} %select_bitcast_fusion), channel_id=1, replica_groups=mesh['ctx'=32,'head'=4] {'ctx'}, use_global_device_ids=true, to_apply=%region_7.8 | all-reduce | flops 6912 | bytes 55296 | tf_op jit(solution)/shard_map/psum | solution.py:34
  425.8 11.4 %fusion.7 = f32[8,1,32,64]{3,1,2,0:T(1,128)S(1)} fusion(f32[8,128]{1,0:T(8,128)S(1)} %get-tuple-element.191, f32[8,32,64]{2,1,0:T(8,128)S(1)} %get-tuple-element.213, f32[32,64,128]{2,1,0:T(8,128)} %all-reduce.3.cloned.1.call-done, f32[8]{0:T(128)S(1)} %get-tuple-element.207, f32[8,32]{1,0:T(8,128)S(1)} %get-tuple-element.152, ...), kind=kOutput, calls=%fused_computation.13 | convolution fusion | flops 33554432 | bytes 1186848 | tf_op jit(solution)/shard_map/rn,rhdn->rhd/dot_general | solution.py:157
  437.2 14.7 %fusion.8 = f32[8,1,32,64]{3,1,2,0:T(1,128)S(1)} fusion(f32[8,128]{1,0:T(8,128)S(1)} %get-tuple-element.208, f32[8,32,64]{2,1,0:T(8,128)S(1)} %get-tuple-element.212, f32[8,32]{1,0:T(8,128)S(1)} %get-tuple-element.180, f32[8,128]{1,0:T(8,128)S(1)} %get-tuple-element.191, f32[8,32,64]{2,1,0:T(8,128)S(1)} %get-tuple-element.213, ...), kind=kOutput, calls=%fused_computation.14 | convolution fusion | flops 39845888 | bytes 1257504 | tf_op jit(solution)/shard_map/rn,rhdn->rhd/dot_general | solution.py:157
  451.9 14.2 %fusion.9 = f32[8,1,32,64]{3,1,2,0:T(1,128)S(1)} fusion(f32[8,128]{1,0:T(8,128)S(1)} %get-tuple-element.195, f32[8,32,64]{2,1,0:T(8,128)S(1)} %get-tuple-element.211, f32[8,32]{1,0:T(8,128)S(1)} %get-tuple-element.182, f32[8,128]{1,0:T(8,128)S(1)} %get-tuple-element.208, f32[8,32,64]{2,1,0:T(8,128)S(1)} %get-tuple-element.212, ...), kind=kOutput, calls=%fused_computation.15 | convolution fusion | flops 46137344 | bytes 1328160 | tf_op jit(solution)/shard_map/rn,rhdn->rhd/dot_general | solution.py:157
  466.1 16.9 %fusion.3 = f32[8,1,32,64]{3,1,2,0:T(1,128)S(1)} fusion(f32[8,128]{1,0:T(8,128)S(1)} %get-tuple-element.197, f32[8,32,64]{2,1,0:T(8,128)S(1)} %get-tuple-element.210, f32[8,32]{1,0:T(8,128)S(1)} %get-tuple-element.184, f32[8,128]{1,0:T(8,128)S(1)} %get-tuple-element.195, f32[8,32,64]{2,1,0:T(8,128)S(1)} %get-tuple-element.211, ...), kind=kOutput, calls=%fused_computation.6 | convolution fusion | flops 52428800 | bytes 1398816 | tf_op jit(solution)/shard_map/rn,rhdn->rhd/dot_general | solution.py:157
  484.4 2.7 convert_element_type.412
  (132 shorter events, 63.5 us)
Async XLA Ops:
  7.2 143.6 %all-gather.4.cloned.1.call-start = ((), (), s32[]{:S(2)}) async-start(), calls=%async_computation.3 | async-start | bytes 34603008 | tf_op jit(solution)/shard_map/all_gather | solution.py:17
  8.3 17.1 %collective-permute-start = (bf16[3,1,2048]{0,2,1:T(8,128)(2,1)S(1)}, bf16[3,1,2048]{0,2,1:T(8,128)(2,1)}, u32[]{:S(2)}, u32[]{:S(2)}) collective-permute-start(bf16[3,1,2048]{0,2,1:T(8,128)(2,1)S(1)} %copy.72), channel_id=1, source_target_pairs={{0,4},{4,8},{8,12},{12,16},{16,20},{20,24},{24,28},{28,32},{32,36}... | collective-permute-start | bytes 36872 | tf_op jit(solution)/shard_map/ppermute | solution.py:12
  11.1 12.6 %collective-permute-start.1 = (bf16[3,1,256]{2,0,1:T(4,128)(2,1)S(1)}, bf16[3,1,256]{2,0,1:T(4,128)(2,1)S(1)}, u32[]{:S(2)}, u32[]{:S(2)}) collective-permute-start(bf16[3,1,256]{2,0,1:T(4,128)(2,1)S(1)} %slice.263), channel_id=1, source_target_pairs={{0,4},{4,8},{8,12},{12,16},{16,20},{20,24},{24,28},{28,32},{32,36}... | collective-permute-start | bytes 4616 | tf_op jit(solution)/shard_map/ppermute | solution.py:12
  15.3 2.4 copy-start.7
  35.0 390.9 %all-reduce.3.cloned.1.call-start = ((), (), s32[]{:S(2)}) async-start(), calls=%async_computation.2 | async-start | bytes 2097152 | tf_op jit(solution)/shard_map/psum | solution.py:34
  150.7 90.1 %copy-start = (f32[32,64,128]{2,1,0:T(8,128)S(1)}, f32[32,64,128]{2,1,0:T(8,128)}, u32[]{:S(2)}) copy-start(f32[32,64,128]{2,1,0:T(8,128)} %fusion.68) | copy-start | bytes 3145732
  242.7 241.6 %reduce-scatter.2.cloned.1.call-start = ((), (), s32[]{:S(2)}) async-start(), calls=%async_computation.1 | async-start | bytes 10485760 | tf_op jit(solution)/shard_map/reduce_scatter | solution.py:115
  242.8 13.2 %copy-start.1 = (bf16[512,1,2048]{0,2,1:T(8,128)(2,1)S(1)}, bf16[512,1,2048]{0,2,1:T(8,128)(2,1)}, u32[]{:S(2)}) copy-start(bf16[512,1,2048]{0,2,1:T(8,128)(2,1)} %copy.84) | copy-start | bytes 6291460
  256.0 14.2 %copy-start.11 = (f32[2048]{0:T(1024)S(1)}, f32[2048]{0:T(1024)}, u32[]{:S(2)}) copy-start(f32[2048]{0:T(1024)} %param.27) | copy-start | bytes 24580
  286.3 138.3 %copy-start.12 = (s32[8]{0:T(128)S(1)}, s32[8]{0:T(128)}, u32[]{:S(2)}) copy-start(s32[8]{0:T(128)} %param.29) | copy-start | bytes 100
  286.3 138.4 %copy-start.2 = (bf16[4,8,2048]{2,1,0:T(8,128)(2,1)S(1)}, bf16[4,8,2048]{2,1,0:T(8,128)(2,1)}, u32[]{:S(2)}) copy-start(bf16[4,8,2048]{2,1,0:T(8,128)(2,1)} %param.30) | copy-start | bytes 393220
  286.3 139.0 %copy-start.4 = (bf16[4,8,256]{2,1,0:T(8,128)(2,1)S(1)}, bf16[4,8,256]{2,1,0:T(8,128)(2,1)}, u32[]{:S(2)}) copy-start(bf16[4,8,256]{2,1,0:T(8,128)(2,1)} %param.32) | copy-start | bytes 49156
  286.3 139.1 %copy-start.5 = (f32[4,8,32]{2,1,0:T(8,128)S(1)}, f32[4,8,32]{2,1,0:T(8,128)}, u32[]{:S(2)}) copy-start(f32[4,8,32]{2,1,0:T(8,128)} %param.33) | copy-start | bytes 12292
  286.4 139.1 %copy-start.6 = (f32[32]{0:T(128)S(1)}, f32[32]{0:T(128)}, u32[]{:S(2)}) copy-start(f32[32]{0:T(128)} %param.22) | copy-start | bytes 388
  286.4 139.1 %copy-start.8 = (f32[32]{0:T(128)S(1)}, f32[32]{0:T(128)}, u32[]{:S(2)}) copy-start(f32[32]{0:T(128)} %copy-done.7) | copy-start | bytes 388
  425.8 11.4 %copy-start.10 = (f32[32,64,128]{2,1,0:T(8,128)S(1)}, f32[32,64,128]{2,1,0:T(8,128)}, u32[]{:S(2)}) copy-start(f32[32,64,128]{2,1,0:T(8,128)} %all-reduce.3.cloned.1.call-done) | copy-start | bytes 3145732
  466.1 16.9 %copy-start.9 = (f32[32]{0:T(128)S(1)}, f32[32]{0:T(128)}, u32[]{:S(2)}) copy-start(f32[32]{0:T(128)} %param.24) | copy-start | bytes 388
  466.1 17.4 %copy-start.3 = (bf16[4,8,2048]{2,1,0:T(8,128)(2,1)S(1)}, bf16[4,8,2048]{2,1,0:T(8,128)(2,1)}, u32[]{:S(2)}) copy-start(bf16[4,8,2048]{2,1,0:T(8,128)(2,1)} %param.31) | copy-start | bytes 393220
Sparse Core Ops, SparseCore 0:
  35.1 115.6 all-gather.3
  242.8 104.4 all-reduce.2
  349.8 80.6 reduce-scatter.1
where the time goes:
time: 496 us; the launch traced here: 494 us
  blocking collectives  172 us (35%)
  matrix products  92.2 us (19%)
  waiting for transfers between devices  84.7 us (17%)
  other arithmetic  73.8 us (15%)
  local copies, waits for them, and re-layouts  50.8 us (10%)
  between operations  14.1 us (3%)
  starting transfers between devices  5.74 us (1%)
    psum x1, blocking collectives, spread(): return lax.psum(jnp.where(mine, value, jnp.zeros_like(value)), axis)  137 us
    all_gather x1, waiting for transfers between devices, prefix(): everything = jax.tree.map(lambda part: lax.all_gather(part, axis), value)  84.6 us
    dot_general x4, matrix products, body(): jnp.einsum('rn,rhdn->rhd', c_step, states, precision=lax.Precision.HIGHEST)  57.1 us
    select_n x32, other arithmetic, step(): return jax.tree.map(lambda a, b: jnp.where(reached, a, b), new, before)  46.7 us
    mul x32, local copies, waits for them, and re-layouts, chain_pair(): later_pair[0][..., None, None] * earlier_pair[1] + later_pair[1]  39.1 us
    all_gather x1, blocking collectives, prefix(): everything = jax.tree.map(lambda part: lax.all_gather(part, axis), value)  24 us
    dot_general x1, matrix products, body(): jnp.einsum('tpi,id->tpd', normed, w_out, preferred_element_type=jnp.float32)  16.1 us
    dot_general x1, matrix products, body(): jnp.einsum('phij,jphd->iphd', mixing, x_heads, preferred_element_type=jnp...  13.2 us
  transfers between devices with their start and end apart: 5, of which 1 were waited for; matrix products, arithmetic and copies ran while one was open for 23% of the time, Pallas kernels for 0%

commit v1 on v0

v1 whole, which is shorter than its diff:
```python
import jax
import jax.numpy as jnp
from jax import lax
from jax.sharding import PartitionSpec as P

norm_eps = 1e-05


def passed_along(value, axis, steps):
    count = lax.axis_size(axis)
    leading, last = (max(0, -steps), min(count, count - steps))
    return lax.ppermute(value, axis, [(source, source + steps) for source in range(leading, last)])


def group_shift(value, axis, count, stride, group, shift):
    pairs = []
    for source in range(count):
        member = (source // stride) % group
        target = source + (((member + shift) % group) - member) * stride
        pairs.append((source, target))
    return lax.ppermute(value, axis, pairs)


def conv_silu(window, weight, length):
    running_sum = jnp.zeros((length,) + window.shape[1:], jnp.float32)
    for offset in range(weight.shape[0]):
        running_sum = running_sum + window[offset : offset + length].astype(jnp.float32) * weight[
            offset
        ].astype(jnp.float32)
    return jax.nn.silu(running_sum).astype(jnp.bfloat16)


def chain(earlier, later):
    return (earlier[0] * later[0], later[0][..., None, None] * earlier[1] + later[1])


def pick(flag, first, second):
    return jax.tree.map(lambda a, b: jnp.where(flag, a, b), first, second)


def ring_scan(own, tails, axis, count, stride, group):
    member = (lax.axis_index(axis) // stride) % group
    received = [None] + [
        group_shift((own, tails), axis, count, stride, group, shift) for shift in range(1, group)
    ]
    identity = (jnp.ones_like(own[0]), jnp.zeros_like(own[1]))
    before = identity
    for shift in range(group - 1, 0, -1):
        before = pick(shift <= member, chain(before, received[shift][0]), before)
    total = chain(before, own)
    for shift in range(group - 1, 0, -1):
        total = pick(shift > member, chain(total, received[shift][0]), total)
    last_tails = tails
    for shift in range(1, group):
        last_tails = pick((member - shift) % group == group - 1, received[shift][1], last_tails)
    return before, total, last_tails


def body(
    x_in,
    z_in,
    bc_in,
    dt_in,
    dt_bias,
    a_log,
    skip,
    conv_x,
    conv_bc,
    norm_gain,
    w_out,
    requests,
    step_x,
    step_z,
    step_bc,
    step_dt,
):
    block_len, prompts, inner_loc = x_in.shape
    heads_loc = dt_in.shape[2]
    head_dim = inner_loc // heads_loc
    state_dim = bc_in.shape[2] // 2
    conv_taps = conv_x.shape[0]
    edge_x, edge_bc = passed_along(
        (x_in[block_len - conv_taps + 1 :], bc_in[block_len - conv_taps + 1 :]), "ctx", 1
    )
    x_conv = conv_silu(jnp.concatenate([edge_x, x_in], axis=0), conv_x, block_len)
    bc_conv = conv_silu(jnp.concatenate([edge_bc, bc_in], axis=0), conv_bc, block_len)
    b_rows = bc_conv[..., :state_dim]
    c_rows = bc_conv[..., state_dim:]
    decay_rates = -jnp.exp(a_log)
    dt_full = jax.nn.softplus(dt_in + dt_bias)
    cum_log = jnp.cumsum(dt_full * decay_rates, axis=0)
    cum_heads = jnp.transpose(cum_log, (1, 2, 0))
    dt_heads = jnp.transpose(dt_full, (1, 2, 0))
    x_heads = x_conv.reshape(block_len, prompts, heads_loc, head_dim)
    block_log = cum_heads[..., -1]
    tail_weights = jnp.transpose(jnp.exp(block_log[..., None] - cum_heads) * dt_heads, (2, 0, 1))
    weighted_x = (x_heads * tail_weights[..., None]).astype(jnp.bfloat16)
    s_local = jnp.einsum("jphd,jpn->phdn", weighted_x, b_rows, preferred_element_type=jnp.float32)
    block_decay = jnp.exp(block_log)

    count = lax.axis_size("ctx")
    here = lax.axis_index("ctx")
    core = here % 2
    tails = (x_in[block_len - conv_taps + 1 :], bc_in[block_len - conv_taps + 1 :])
    own = (block_decay, s_local)
    other, other_tails = group_shift((own, tails), "ctx", count, 1, 2, 1)
    first = pick(core == 0, own, other)
    second = pick(core == 0, other, own)
    chip_total = chain(first, second)
    chip_tails = pick(core == 0, other_tails, tails)
    half = state_dim // 2
    chip_half = (
        chip_total[0],
        jnp.where(core == 0, chip_total[1][..., :half], chip_total[1][..., half:]),
    )
    row_before, row_total, row_tails = ring_scan(chip_half, chip_tails, "ctx", count, 2, 4)
    rows = count // 8
    top_before, top_total, final_tails = ring_scan(row_total, row_tails, "ctx", count, 8, rows)
    chip_before = chain(top_before, row_before)
    mine = (chip_before[1], top_total[1])
    theirs = group_shift(mine, "ctx", count, 1, 2, 1)
    joined = jax.tree.map(
        lambda a, b: jnp.where(core == 0, jnp.concatenate([a, b], -1), jnp.concatenate([b, a], -1)),
        mine,
        theirs,
    )
    chip_state, final_state = joined
    s_before = jnp.where(
        core == 0, chip_state, first[0][..., None, None] * chip_state + first[1]
    )

    scores = jnp.einsum("ipn,jpn->pij", c_rows, b_rows, preferred_element_type=jnp.float32)
    position = lax.iota(jnp.int32, block_len)
    causal = position[:, None] >= position[None, :]
    gaps = jnp.where(causal, cum_heads[..., :, None] - cum_heads[..., None, :], -jnp.inf)
    mixing = (scores[:, None] * jnp.exp(gaps) * dt_heads[..., None, :]).astype(jnp.bfloat16)
    y_intra = jnp.einsum("phij,jphd->iphd", mixing, x_heads, preferred_element_type=jnp.float32)
    y_inter = (
        jnp.einsum(
            "ipn,phdn->iphd", c_rows.astype(jnp.float32), s_before, precision=lax.Precision.HIGHEST
        )
        * jnp.exp(cum_log)[..., None]
    )
    y_all = y_intra + y_inter + skip[:, None] * x_heads.astype(jnp.float32)
    gated_out = y_all.reshape(block_len, prompts, inner_loc) * jax.nn.silu(z_in.astype(jnp.float32))
    square_sums = lax.psum(jnp.sum(gated_out * gated_out, axis=-1), "head")
    inner_total = inner_loc * lax.axis_size("head")
    normed = (
        gated_out * lax.rsqrt(square_sums / inner_total + norm_eps)[..., None] * norm_gain
    ).astype(jnp.bfloat16)
    projected = lax.psum_scatter(
        jnp.einsum("tpi,id->tpd", normed, w_out, preferred_element_type=jnp.float32),
        "head",
        scatter_dimension=0,
        tiled=True,
    )
    out = projected.astype(jnp.bfloat16)

    final_x, final_bc = final_tails
    slot_count = requests.shape[0]
    steps = step_x.shape[0]
    slot_pick = (requests[:, None] == lax.iota(jnp.int32, prompts)[None, :]).astype(jnp.float32)
    live_slots = requests < prompts
    hist_x = jnp.einsum(
        "rp,kpi->kri", slot_pick, final_x.astype(jnp.float32), precision=lax.Precision.HIGHEST
    ).astype(jnp.bfloat16)
    hist_bc = jnp.einsum(
        "rp,kpi->kri", slot_pick, final_bc.astype(jnp.float32), precision=lax.Precision.HIGHEST
    ).astype(jnp.bfloat16)
    window_x = jnp.concatenate([hist_x, step_x], axis=0)
    window_bc = jnp.concatenate([hist_bc, step_bc], axis=0)
    new_x = conv_silu(window_x, conv_x, steps)
    new_bc = conv_silu(window_bc, conv_bc, steps)
    dt_step = jax.nn.softplus(step_dt + dt_bias)
    x_step = new_x.reshape(steps, slot_count, heads_loc, head_dim).astype(jnp.float32)
    b_step = new_bc[..., :state_dim].astype(jnp.float32)
    c_step = new_bc[..., state_dim:].astype(jnp.float32)
    step_decay = jnp.exp(dt_step * decay_rates)
    pushed = dt_step[..., None] * x_step
    from_final = jnp.einsum(
        "phdn,srn->psrhd", final_state.reshape(prompts, heads_loc, head_dim, state_dim), c_step,
        precision=lax.Precision.HIGHEST,
    )
    from_final = jnp.einsum("rp,psrhd->srhd", slot_pick, from_final, precision=lax.Precision.HIGHEST)
    overlap = jnp.einsum("trn,srn->tsr", b_step, c_step, precision=lax.Precision.HIGHEST)
    outputs = []
    carried = jnp.ones_like(step_decay[0])
    for step_index in range(steps):
        carried = carried * step_decay[step_index]
        y_step = carried[..., None] * from_final[step_index]
        for earlier in range(step_index + 1):
            weight = jnp.ones_like(step_decay[0])
            for later in range(earlier + 1, step_index + 1):
                weight = weight * step_decay[later]
            y_step = y_step + (weight * overlap[earlier, step_index][:, None])[..., None] * pushed[
                earlier
            ]
        y_step = y_step + skip[:, None] * x_step[step_index]
        gated_step = y_step.reshape(slot_count, inner_loc) * jax.nn.silu(
            step_z[step_index].astype(jnp.float32)
        )
        outputs.append(jnp.where(live_slots[:, None], gated_step, 0.0).astype(jnp.bfloat16))
    return (out, jnp.stack(outputs))

def solution(mesh):
    placed = (
        P("ctx", None, "head"),
        P("ctx", None, "head"),
        P("ctx", None, None),
        P("ctx", None, "head"),
        P("head"),
        P("head"),
        P("head"),
        P(None, "head"),
        P(),
        P("head"),
        P("head", None),
        P("ctx"),
        P(None, "ctx", "head"),
        P(None, "ctx", "head"),
        P(None, "ctx", None),
        P(None, "ctx", "head"),
    )
    return jax.shard_map(
        body,
        mesh=mesh,
        in_specs=placed,
        out_specs=(P(("ctx", "head"), None, None), P(None, "ctx", "head")),
        check_vma=False,
    )
```

time: 496 us -> 289 us (0.58)
  blocking collectives: 172 us -> 12 us
  matrix products: 92.2 us -> 32.7 us
  waiting for transfers between devices: 84.7 us -> 129 us
  other arithmetic: 73.8 us -> 36.6 us
  starting transfers between devices: 5.74 us -> 42.9 us
  local copies, waits for them, and re-layouts: 50.8 us -> 18.5 us
    psum x1 -> x0, blocking collectives: 137 us -> none  [spread(): return lax.psum(jnp.where(mine, value, jnp.zeros_like(value)), axis)]
    ppermute x0 -> x30, waiting for transfers between devices: none -> 129 us  [group_shift(): return lax.ppermute(value, axis, pairs)]
    all_gather x1 -> x0, waiting for transfers between devices: 84.6 us -> none  [prefix(): everything = jax.tree.map(lambda part: lax.all_gather(part, axis), value)]
    dot_general x4 -> x2, matrix products: 57.1 us -> 3.34 us  [the longest x1 3.22 us: body(): jnp.einsum('phdn,srn->psrhd', final_state.reshape(prompts, heads_loc, hea...]
    select_n x32 -> x8, other arithmetic: 46.7 us -> 6.35 us  [the longest x7 6.01 us: pick(): return jax.tree.map(lambda a, b: jnp.where(flag, a, b), first, second)]
    ppermute x0 -> x30, starting transfers between devices: none -> 37.2 us  [group_shift(): return lax.ppermute(value, axis, pairs)]
    mul x32 -> x23, local copies, waits for them, and re-layouts: 39.1 us -> 5.8 us  [the longest x12 4.32 us: body(): (weight * overlap[earlier, step_index][:, None])[..., None]]
    all_gather x1 -> x0, blocking collectives: 24 us -> none  [prefix(): everything = jax.tree.map(lambda part: lax.all_gather(part, axis), value)]
  transfers between devices with their start and end apart: 5 -> 33, of which waited for: 1 -> 17; matrix products, arithmetic and copies ran while one was open for 23% -> 15% of each run, Pallas kernels for 0% -> 0%
where the time goes in v1:
time: 289 us; the launch traced here: 287 us
  waiting for transfers between devices  129 us (45%)
  starting transfers between devices  42.9 us (15%)
  other arithmetic  36.6 us (13%)
  matrix products  32.7 us (11%)
  local copies, waits for them, and re-layouts  18.5 us (6%)
  between operations  15.1 us (5%)
  blocking collectives  12 us (4%)
    ppermute x30, waiting for transfers between devices, group_shift(): return lax.ppermute(value, axis, pairs)  129 us
    ppermute x30, starting transfers between devices, group_shift(): return lax.ppermute(value, axis, pairs)  37.2 us
    dot_general x1, matrix products, body(): jnp.einsum('tpi,id->tpd', normed, w_out, preferred_element_type=jnp.float32)  16.1 us
    psum x1, blocking collectives, body(): square_sums = lax.psum(jnp.sum(gated_out * gated_out, axis=-1), 'head')  12 us
    dot_general x1, matrix products, body(): jnp.einsum('phij,jphd->iphd', mixing, x_heads, preferred_element_type=jnp...  9.63 us
    unnamed x111, local copies, waits for them, and re-layouts  7.86 us
    convert_element_type x1, other arithmetic, body(): weighted_x = (x_heads * tail_weights[..., None]).astype(jnp.bfloat16)  7.33 us
    add x2, other arithmetic, chain(): later[0][..., None, None] * earlier[1] + later[1]  6.11 us
  transfers between devices with their start and end apart: 33, of which 17 were waited for; matrix products, arithmetic and copies ran while one was open for 15% of the time, Pallas kernels for 0%

profile of v1, /device:TPU:0, one launch (start us, length us, event | category | flops | bytes accessed | tf_op | source)
XLA Modules:
  0.0 287.0 jit_solution(10003651989013036885)
XLA Ops:
  7.3 2.9 %copy.44 = bf16[512,1,2048]{0,2,1:T(8,128)(2,1)S(1)} copy(bf16[512,1,2048]{2,0,1:T(8,128)(2,1)} %param.16) | data formatting | bytes 4194304 | tf_op args[0]
  10.4 2.1 collective-permute-start
  12.5 3.5 %collective-permute-start.1 = (bf16[3,1,256]{2,0,1:T(4,128)(2,1)S(1)}, bf16[3,1,256]{2,0,1:T(4,128)(2,1)S(1)}, u32[]{:S(2)}, u32[]{:S(2)}) collective-permute-start(bf16[3,1,256]{2,0,1:T(4,128)(2,1)S(1)} %slice.221), channel_id=1, source_target_pairs={{0,4},{4,8},{8,12},{12,16},{16,20},{20,24},{24,28},{28,32},{32,36}... | collective-permute-start | bytes 4616 | tf_op jit(solution)/shard_map/ppermute | solution.py:12
  16.9 1.2 reduce-window.6
  20.4 7.3 %fusion.8 = (bf16[512,1,2048]{0,2,1:T(8,128)(2,1)S(1)}, bf16[512,1,2048]{0,2,1:T(8,128)(2,1)}) fusion(f32[2048]{0:T(1024)S(1)} %bitcast.219, bf16[512,1,2048]{0,2,1:T(8,128)(2,1)S(1)} %copy.44, f32[2048]{0:T(1024)S(1)} %bitcast.221, bf16[3,1,2048]{0,2,1:T(8,128)(2,1)} %collective-permute-done, f32[2048]{0:T(1024)S(1)} %bitcast.217, f32[2048]{0:T(1024)S(1)} %bitcast.215, ...), kind=kLoop, calls=%fused_computation.14 | loop fusion | flops 29360128 | bytes 10530816 | tf_op jit(solution)/shard_map/convert_element_type | solution.py:97
  30.1 1.5 bitcast_add_fusion
  32.4 1.4 select_add_fusion
  34.2 4.3 %collective-permute-start.10 = (f32[1,32,64,64]{3,2,1,0:T(8,128)S(1)}, f32[1,32,64,64]{3,2,1,0:T(8,128)S(1)}, u32[]{:S(2)}, u32[]{:S(2)}) collective-permute-start(f32[1,32,64,64]{3,2,1,0:T(8,128)S(1)} %slice_select_fusion), channel_id=1, source_target_pairs={{0,24},{4,28},{8,0},{12,4},{16,8},{20,12},{24,16},{28,20},{32,56},... | collective-permute-start | bytes 1572872 | tf_op jit(solution)/shard_map/ppermute | solution.py:21
  39.2 1.0 collective-permute-start.12
  41.0 2.3 collective-permute-start.3
  43.4 40.4 %collective-permute-done.3 = f32[1,32]{1,0:T(1,128)S(1)} collective-permute-done((f32[1,32]{1,0:T(1,128)S(1)}, f32[1,32]{1,0:T(1,128)S(1)}, u32[]{:S(2)}, u32[]{:S(2)}) %collective-permute-start.3) | collective-permute-done | bytes 160 | tf_op jit(solution)/shard_map/ppermute | solution.py:21
  83.8 2.6 collective-permute-start.4
  86.4 1.1 collective-permute-done.5
  87.5 1.3 collective-permute-done.4
  88.9 2.0 add_select_fusion.2
  90.9 4.3 %collective-permute-start.13 = (f32[1,32,64,64]{3,2,1,0:T(8,128)}, f32[1,32,64,64]{3,2,1,0:T(8,128)}, u32[]{:S(2)}, u32[]{:S(2)}) collective-permute-start(f32[1,32,64,64]{3,2,1,0:T(8,128)} %add_select_fusion.2), channel_id=1, source_target_pairs={{0,96},{4,100},{8,104},{12,108},{16,112},{20,116},{24,120},{28,124... | collective-permute-start | bytes 1572872 | tf_op jit(solution)/shard_map/ppermute | solution.py:21
  97.0 2.4 collective-permute-start.8
  99.4 3.9 %copy.53 = bf16[512,1,2048]{0,2,1:T(8,128)(2,1)} copy(bf16[512,1,2048]{2,0,1:T(8,128)(2,1)} %param.17) | data formatting | bytes 4194304 | tf_op args[1]
  103.3 35.4 %collective-permute-done.8 = f32[1,32]{1,0:T(1,128)S(1)} collective-permute-done((f32[1,32]{1,0:T(1,128)S(1)}, f32[1,32]{1,0:T(1,128)S(1)}, u32[]{:S(2)}, u32[]{:S(2)}) %collective-permute-start.8) | collective-permute-done | bytes 160 | tf_op jit(solution)/shard_map/ppermute | solution.py:21
  138.7 2.7 collective-permute-start.7
  142.5 1.4 collective-permute-done.7
  143.8 4.7 %multiply_add_fusion = f32[1,32,64,64]{3,2,1,0:T(8,128)S(1)} fusion(f32[1,32,64,64]{3,2,1,0:T(8,128)} %collective-permute-done.15, f32[1,32,64,64]{3,2,1,0:T(8,128)} %collective-permute-done.14, f32[1,32,64,64]{3,2,1,0:T(8,128)} %collective-permute-done.13, f32[1,32,64,64]{3,2,1,0:T(8,128)} %copy-done.4, f32[1,32,64,64]{3,2,1,0:T(8,128)} %copy-done.3, ...), kind=kLoop, calls=%fused_computation.45 | loop fusion | flops 2359296 | bytes 3670918 | tf_op jit(solution)/shard_map/add | solution.py:34
  148.7 9.6 %fusion = f32[32,64,512]{2,1,0:T(8,128)S(1)} fusion(bf16[512,32,64]{0,2,1:T(8,128)(2,1)S(1)} %bitcast.204, f32[32,512]{1,0:T(8,128)S(1)} %copy-done.23, f32[32,512]{1,0:T(8,128)S(1)} %copy-done.24, f32[512,512]{1,0:T(8,128)S(1)} %fusion.35, pred[512,512]{1,0:T(8,128)(4,1)S(1)} %copy-done.15), kind=kOutput, calls=%fused_computation.1 | convolution fusion | flops 1115684864 | bytes 7733248 | tf_op jit(solution)/shard_map/phij,jphd->iphd/dot_general | solution.py:137
  158.4 2.7 fusion.7
  161.1 3.5 %multiply_reduce_fusion = (f32[512]{0:T(512)S(1)}, f32[512,1,2048]{0,2,1:T(8,128)}) fusion(bf16[512,1,2048]{0,2,1:T(8,128)(2,1)S(1)} %copy-done.1, f32[512,1,32,64]{0,3,2,1:T(8,128)S(1)} %fusion.7), kind=kLoop, calls=%fused_computation.16 | loop fusion | flops 8388096 | bytes 10487808 | tf_op jit(solution)/shard_map/reduce_sum | solution.py:146
  164.6 12.0 %psum.7 = f32[512,1]{0,1:T(1,128)S(1)} all-reduce(f32[512,1]{0,1:T(1,128)S(1)} %bitcast.232), channel_id=1, replica_groups=mesh['ctx'=32,'head'=4] {'head'}, use_global_device_ids=true, to_apply=%region_3.4 | all-reduce | flops 512 | bytes 4096 | tf_op jit(solution)/shard_map/psum | solution.py:146
  176.6 16.1 %convolution_bitcast_fusion = f32[512,1,4096]{2,0,1:T(8,128)} fusion(bf16[2048,4096]{1,0:T(8,128)(2,1)} %param.26, f32[512,1,2048]{0,2,1:T(8,128)} %get-tuple-element.20, f32[2048]{0:T(1024)S(1)} %copy-done.51, f32[512]{0:T(512)S(1)} %bitcast.240), kind=kOutput, calls=%fused_computation.3 | convolution fusion | flops 8593080320 | bytes 29370368 | tf_op jit(solution)/shard_map/tpi,id->tpd/dot_general | solution.py:152
  195.7 1.7 collective-permute-start.18
  197.5 0.9 collective-permute-start.20
  198.4 0.9 collective-permute-done.18
  199.3 3.2 %collective-permute-done.19 = bf16[3,1,256]{2,0,1:T(4,128)(2,1)S(1)} collective-permute-done((bf16[3,1,256]{2,0,1:T(4,128)(2,1)S(1)}, bf16[3,1,256]{2,0,1:T(4,128)(2,1)S(1)}, u32[]{:S(2)}, u32[]{:S(2)}) %collective-permute-start.19) | collective-permute-done | bytes 1568 | tf_op jit(solution)/shard_map/ppermute | solution.py:21
  202.6 3.4 %collective-permute-start.21 = (bf16[3,1,256]{2,0,1:T(4,128)(2,1)S(1)}, bf16[3,1,256]{2,0,1:T(4,128)(2,1)S(1)}, u32[]{:S(2)}, u32[]{:S(2)}) collective-permute-start(bf16[3,1,256]{2,0,1:T(4,128)(2,1)S(1)} %select_select_fusion.1), channel_id=1, source_target_pairs={{0,96},{4,100},{8,104},{12,108},{16,112},{20,116},{24,120},{28,124... | collective-permute-start | bytes 4616 | tf_op jit(solution)/shard_map/ppermute | solution.py:21
  206.0 0.9 collective-permute-start.23
  207.8 3.2 %collective-permute-done.22 = bf16[3,1,256]{2,0,1:T(4,128)(2,1)S(1)} collective-permute-done((bf16[3,1,256]{2,0,1:T(4,128)(2,1)S(1)}, bf16[3,1,256]{2,0,1:T(4,128)(2,1)S(1)}, u32[]{:S(2)}, u32[]{:S(2)}) %collective-permute-start.22) | collective-permute-done | bytes 1568 | tf_op jit(solution)/shard_map/ppermute | solution.py:21
  212.4 1.9 collective-permute-start.26
  215.9 11.3 %collective-permute-done.26 = bf16[3,1,2048]{0,2,1:T(8,128)(2,1)S(1)} collective-permute-done((bf16[3,1,2048]{0,2,1:T(8,128)(2,1)S(1)}, bf16[3,1,2048]{0,2,1:T(8,128)(2,1)S(1)}, u32[]{:S(2)}, u32[]{:S(2)}) %collective-permute-start.26) | collective-permute-done | bytes 12320 | tf_op jit(solution)/shard_map/ppermute | solution.py:21
  227.3 3.3 %collective-permute-done.27 = bf16[3,1,2048]{0,2,1:T(8,128)(2,1)S(1)} collective-permute-done((bf16[3,1,2048]{0,2,1:T(8,128)(2,1)S(1)}, bf16[3,1,2048]{0,2,1:T(8,128)(2,1)S(1)}, u32[]{:S(2)}, u32[]{:S(2)}) %collective-permute-start.27) | collective-permute-done | bytes 12320 | tf_op jit(solution)/shard_map/ppermute | solution.py:21
  230.6 7.4 %collective-permute-done.28 = bf16[3,1,2048]{0,2,1:T(8,128)(2,1)S(1)} collective-permute-done((bf16[3,1,2048]{0,2,1:T(8,128)(2,1)S(1)}, bf16[3,1,2048]{0,2,1:T(8,128)(2,1)S(1)}, u32[]{:S(2)}, u32[]{:S(2)}) %collective-permute-start.28) | collective-permute-done | bytes 12320 | tf_op jit(solution)/shard_map/ppermute | solution.py:21
  238.1 0.9 collective-permute-start.29
  239.0 1.3 collective-permute-start.30
  240.3 1.3 collective-permute-start.31
  246.6 6.3 %collective-permute-done.29 = bf16[3,1,2048]{0,2,1:T(8,128)(2,1)S(1)} collective-permute-done((bf16[3,1,2048]{0,2,1:T(8,128)(2,1)S(1)}, bf16[3,1,2048]{0,2,1:T(8,128)(2,1)S(1)}, u32[]{:S(2)}, u32[]{:S(2)}) %collective-permute-start.29) | collective-permute-done | bytes 12320 | tf_op jit(solution)/shard_map/ppermute | solution.py:21
  253.0 2.4 collective-permute-done.30
  255.4 10.1 %collective-permute-done.31 = bf16[3,1,2048]{0,2,1:T(8,128)(2,1)S(1)} collective-permute-done((bf16[3,1,2048]{0,2,1:T(8,128)(2,1)S(1)}, bf16[3,1,2048]{0,2,1:T(8,128)(2,1)S(1)}, u32[]{:S(2)}, u32[]{:S(2)}) %collective-permute-start.31) | collective-permute-done | bytes 12320 | tf_op jit(solution)/shard_map/ppermute | solution.py:21
  266.6 2.9 %add_select_fusion = f32[1,32,64,64]{3,2,1,0:T(8,128)S(1)} fusion(f32[1,32,64,64]{3,2,1,0:T(8,128)} %collective-permute-done.15, f32[1,32,64,64]{3,2,1,0:T(8,128)} %collective-permute-done.14, f32[1,32,64,64]{3,2,1,0:T(8,128)} %collective-permute-done.13, f32[1,32,64,64]{3,2,1,0:T(8,128)} %add_select_fusion.2, f32[32]{0:T(128)} %bitcast.245, ...), kind=kLoop, calls=%fused_computation.41 | loop fusion | flops 2490368 | bytes 2622086 | tf_op jit(solution)/shard_map/jit(_where)/select_n | solution.py:38
  270.1 1.2 fusion.38
  272.7 3.2 %convolution_multiply_fusion = f32[4,8,32,64]{3,1,2,0:T(8,128)S(1)} fusion(f32[32,64,64]{2,1,0:T(8,128)} %bitcast.55, f32[32,64,64]{2,1,0:T(8,128)S(1)} %bitcast.207, pred[]{:T(512)S(6)} %eq.41, f32[8]{0:T(128)S(1)} %copy-done.39, bf16[4,8,256]{2,1,0:T(8,128)(2,1)S(1)} %multiply_convert_fusion.7), kind=kOutput, calls=%fused_computation.29 | convolution fusion | flops 101515264 | bytes 1843713 | tf_op jit(solution)/shard_map/phdn,srn->psrhd/dot_general | solution.py:180
  277.5 2.7 convert_element_type.218
  (234 shorter events, 27.4 us)
Async XLA Ops:
  7.2 12.1 %copy-start.25 = (bf16[4,2048]{1,0:T(4,128)(2,1)S(1)}, bf16[4,2048]{1,0:T(4,128)(2,1)}, u32[]{:S(2)}) copy-start(bf16[4,2048]{1,0:T(4,128)(2,1)} %param.23) | copy-start | bytes 49156
  7.2 12.2 %copy-start.36 = (bf16[4,256]{1,0:T(4,128)(2,1)S(1)}, bf16[4,256]{1,0:T(4,128)(2,1)}, u32[]{:S(2)}) copy-start(bf16[4,256]{1,0:T(4,128)(2,1)} %param.24) | copy-start | bytes 6148
  7.2 270.3 %reduce-scatter.2.cloned.1.call-start = ((), (), s32[]{:S(2)}) async-start(), calls=%async_computation.1 | async-start | bytes 10485760 | tf_op jit(solution)/shard_map/reduce_scatter | solution.py:151
  10.4 17.3 %copy-start.7 = (bf16[3,1,2048]{0,2,1:T(8,128)(2,1)}, bf16[3,1,2048]{0,2,1:T(8,128)(2,1)S(1)}, u32[]{:S(2)}) copy-start(bf16[3,1,2048]{0,2,1:T(8,128)(2,1)S(1)} %slice.274) | copy-start | bytes 36868
  10.4 9.4 %collective-permute-start = (bf16[3,1,2048]{0,2,1:T(8,128)(2,1)S(1)}, bf16[3,1,2048]{0,2,1:T(8,128)(2,1)}, u32[]{:S(2)}, u32[]{:S(2)}) collective-permute-start(bf16[3,1,2048]{0,2,1:T(8,128)(2,1)S(1)} %slice.274), channel_id=1, source_target_pairs={{0,4},{4,8},{8,12},{12,16},{16,20},{20,24},{24,28},{28,32},{32,36}... | collective-permute-start | bytes 36872 | tf_op jit(solution)/shard_map/ppermute | solution.py:12
  12.5 7.0 %collective-permute-start.1 = (bf16[3,1,256]{2,0,1:T(4,128)(2,1)S(1)}, bf16[3,1,256]{2,0,1:T(4,128)(2,1)S(1)}, u32[]{:S(2)}, u32[]{:S(2)}) collective-permute-start(bf16[3,1,256]{2,0,1:T(4,128)(2,1)S(1)} %slice.221), channel_id=1, source_target_pairs={{0,4},{4,8},{8,12},{12,16},{16,20},{20,24},{24,28},{28,32},{32,36}... | collective-permute-start | bytes 4616 | tf_op jit(solution)/shard_map/ppermute | solution.py:12
  28.5 3.9 %collective-permute-start.9 = (f32[1,32,64,128]{3,2,1,0:T(8,128)S(1)}, f32[1,32,64,128]{3,2,1,0:T(8,128)}, u32[]{:S(2)}, u32[]{:S(2)}) collective-permute-start(f32[1,32,64,128]{3,2,1,0:T(8,128)S(1)} %convolution_bitcast_fusion.1), channel_id=1, source_target_pairs={{0,4},{4,0},{8,12},{12,8},{16,20},{20,16},{24,28},{28,24},{32,36},... | collective-permute-start | bytes 3145736 | tf_op jit(solution)/shard_map/ppermute | solution.py:21
  29.4 2.4 collective-permute-start.2
  30.1 10.8 %copy-start.6 = (f32[32,1,4,128]{3,2,1,0:T(4,128)S(1)}, f32[32,1,4,128]{3,2,1,0:T(4,128)}, u32[]{:S(2)}) copy-start(f32[32,1,4,128]{3,2,1,0:T(4,128)} %copy-done.5) | copy-start | bytes 196612
  34.2 54.6 %collective-permute-start.10 = (f32[1,32,64,64]{3,2,1,0:T(8,128)S(1)}, f32[1,32,64,64]{3,2,1,0:T(8,128)S(1)}, u32[]{:S(2)}, u32[]{:S(2)}) collective-permute-start(f32[1,32,64,64]{3,2,1,0:T(8,128)S(1)} %slice_select_fusion), channel_id=1, source_target_pairs={{0,24},{4,28},{8,0},{12,4},{16,8},{20,12},{24,16},{28,20},{32,56},... | collective-permute-start | bytes 1572872 | tf_op jit(solution)/shard_map/ppermute | solution.py:21
  38.5 50.3 %collective-permute-start.11 = (f32[1,32,64,64]{3,2,1,0:T(8,128)S(1)}, f32[1,32,64,64]{3,2,1,0:T(8,128)S(1)}, u32[]{:S(2)}, u32[]{:S(2)}) collective-permute-start(f32[1,32,64,64]{3,2,1,0:T(8,128)S(1)} %slice_select_fusion), channel_id=1, source_target_pairs={{0,16},{4,20},{8,24},{12,28},{16,0},{20,4},{24,8},{28,12},{32,48},... | collective-permute-start | bytes 1572872 | tf_op jit(solution)/shard_map/ppermute | solution.py:21
  39.2 49.7 %collective-permute-start.12 = (f32[1,32,64,64]{3,2,1,0:T(8,128)S(1)}, f32[1,32,64,64]{3,2,1,0:T(8,128)S(1)}, u32[]{:S(2)}, u32[]{:S(2)}) collective-permute-start(f32[1,32,64,64]{3,2,1,0:T(8,128)S(1)} %slice_select_fusion), channel_id=1, source_target_pairs={{0,8},{4,12},{8,16},{12,20},{16,24},{20,28},{24,0},{28,4},{32,40},... | collective-permute-start | bytes 1572872 | tf_op jit(solution)/shard_map/ppermute | solution.py:21
  41.0 42.7 %collective-permute-start.3 = (f32[1,32]{1,0:T(1,128)S(1)}, f32[1,32]{1,0:T(1,128)S(1)}, u32[]{:S(2)}, u32[]{:S(2)}) collective-permute-start(f32[1,32]{1,0:T(1,128)S(1)} %get-tuple-element.59), channel_id=1, source_target_pairs={{0,24},{4,28},{8,0},{12,4},{16,8},{20,12},{24,16},{28,20},{32,56},... | collective-permute-start | bytes 392 | tf_op jit(solution)/shard_map/ppermute | solution.py:21
  43.4 44.2 %collective-permute-start.5 = (f32[1,32]{1,0:T(1,128)S(1)}, f32[1,32]{1,0:T(1,128)S(1)}, u32[]{:S(2)}, u32[]{:S(2)}) collective-permute-start(f32[1,32]{1,0:T(1,128)S(1)} %get-tuple-element.59), channel_id=1, source_target_pairs={{0,8},{4,12},{8,16},{12,20},{16,24},{20,28},{24,0},{28,4},{32,40},... | collective-permute-start | bytes 392 | tf_op jit(solution)/shard_map/ppermute | solution.py:21
  83.8 5.1 %collective-permute-start.4 = (f32[1,32]{1,0:T(1,128)S(1)}, f32[1,32]{1,0:T(1,128)S(1)}, u32[]{:S(2)}, u32[]{:S(2)}) collective-permute-start(f32[1,32]{1,0:T(1,128)S(1)} %get-tuple-element.59), channel_id=1, source_target_pairs={{0,16},{4,20},{8,24},{12,28},{16,0},{20,4},{24,8},{28,12},{32,48},... | collective-permute-start | bytes 392 | tf_op jit(solution)/shard_map/ppermute | solution.py:21
  90.9 52.9 %collective-permute-start.13 = (f32[1,32,64,64]{3,2,1,0:T(8,128)}, f32[1,32,64,64]{3,2,1,0:T(8,128)}, u32[]{:S(2)}, u32[]{:S(2)}) collective-permute-start(f32[1,32,64,64]{3,2,1,0:T(8,128)} %add_select_fusion.2), channel_id=1, source_target_pairs={{0,96},{4,100},{8,104},{12,108},{16,112},{20,116},{24,120},{28,124... | collective-permute-start | bytes 1572872 | tf_op jit(solution)/shard_map/ppermute | solution.py:21
  95.2 48.6 %collective-permute-start.14 = (f32[1,32,64,64]{3,2,1,0:T(8,128)}, f32[1,32,64,64]{3,2,1,0:T(8,128)}, u32[]{:S(2)}, u32[]{:S(2)}) collective-permute-start(f32[1,32,64,64]{3,2,1,0:T(8,128)} %add_select_fusion.2), channel_id=1, source_target_pairs={{0,64},{4,68},{8,72},{12,76},{16,80},{20,84},{24,88},{28,92},{32,9... | collective-permute-start | bytes 1572872 | tf_op jit(solution)/shard_map/ppermute | solution.py:21
  96.0 47.8 %collective-permute-start.15 = (f32[1,32,64,64]{3,2,1,0:T(8,128)}, f32[1,32,64,64]{3,2,1,0:T(8,128)}, u32[]{:S(2)}, u32[]{:S(2)}) collective-permute-start(f32[1,32,64,64]{3,2,1,0:T(8,128)} %add_select_fusion.2), channel_id=1, source_target_pairs={{0,32},{4,36},{8,40},{12,44},{16,48},{20,52},{24,56},{28,60},{32,6... | collective-permute-start | bytes 1572872 | tf_op jit(solution)/shard_map/ppermute | solution.py:21
  96.9 51.6 %copy-start.49 = (f32[1,32]{1,0:T(1,128)}, f32[1,32]{1,0:T(1,128)S(1)}, u32[]{:S(2)}) copy-start(f32[1,32]{1,0:T(1,128)S(1)} %get-tuple-element.21) | copy-start | bytes 388
  97.0 41.8 %collective-permute-start.8 = (f32[1,32]{1,0:T(1,128)S(1)}, f32[1,32]{1,0:T(1,128)S(1)}, u32[]{:S(2)}, u32[]{:S(2)}) collective-permute-start(f32[1,32]{1,0:T(1,128)S(1)} %get-tuple-element.21), channel_id=1, source_target_pairs={{0,96},{4,100},{8,104},{12,108},{16,112},{20,116},{24,120},{28,124... | collective-permute-start | bytes 392 | tf_op jit(solution)/shard_map/ppermute | solution.py:21
  103.3 39.2 %collective-permute-start.6 = (f32[1,32]{1,0:T(1,128)S(1)}, f32[1,32]{1,0:T(1,128)S(1)}, u32[]{:S(2)}, u32[]{:S(2)}) collective-permute-start(f32[1,32]{1,0:T(1,128)S(1)} %get-tuple-element.21), channel_id=1, source_target_pairs={{0,32},{4,36},{8,40},{12,44},{16,48},{20,52},{24,56},{28,60},{32,6... | collective-permute-start | bytes 392 | tf_op jit(solution)/shard_map/ppermute | solution.py:21
  138.7 9.8 %copy-start.50 = (f32[1,32]{1,0:T(1,128)}, f32[1,32]{1,0:T(1,128)S(1)}, u32[]{:S(2)}) copy-start(f32[1,32]{1,0:T(1,128)S(1)} %collective-permute-done.8) | copy-start | bytes 388
  138.7 5.1 %collective-permute-start.7 = (f32[1,32]{1,0:T(1,128)S(1)}, f32[1,32]{1,0:T(1,128)S(1)}, u32[]{:S(2)}, u32[]{:S(2)}) collective-permute-start(f32[1,32]{1,0:T(1,128)S(1)} %get-tuple-element.21), channel_id=1, source_target_pairs={{0,64},{4,68},{8,72},{12,76},{16,80},{20,84},{24,88},{28,92},{32,9... | collective-permute-start | bytes 392 | tf_op jit(solution)/shard_map/ppermute | solution.py:21
  142.5 15.9 %copy-start.46 = (f32[1,32]{1,0:T(1,128)}, f32[1,32]{1,0:T(1,128)S(1)}, u32[]{:S(2)}) copy-start(f32[1,32]{1,0:T(1,128)S(1)} %collective-permute-done.6) | copy-start | bytes 388
  143.8 14.5 %copy-start.47 = (f32[1,32]{1,0:T(1,128)}, f32[1,32]{1,0:T(1,128)S(1)}, u32[]{:S(2)}) copy-start(f32[1,32]{1,0:T(1,128)S(1)} %collective-permute-done.7) | copy-start | bytes 388
  148.6 9.8 %collective-permute-start.16 = (f32[1,32,64,64]{3,2,1,0:T(8,128)S(1)}, f32[1,32,64,64]{3,2,1,0:T(8,128)S(1)}, u32[]{:S(2)}, u32[]{:S(2)}) collective-permute-start(f32[1,32,64,64]{3,2,1,0:T(8,128)S(1)} %multiply_add_fusion), channel_id=1, source_target_pairs={{0,4},{4,0},{8,12},{12,8},{16,20},{20,16},{24,28},{28,24},{32,36},... | collective-permute-start | bytes 1572872 | tf_op jit(solution)/shard_map/ppermute | solution.py:21
  161.1 15.5 %copy-start.51 = (f32[2048]{0:T(1024)S(1)}, f32[2048]{0:T(1024)}, u32[]{:S(2)}) copy-start(f32[2048]{0:T(1024)} %param.25) | copy-start | bytes 24580
  192.7 18.5 %copy-start.27 = (bf16[4,8,256]{2,1,0:T(8,128)(2,1)S(1)}, bf16[4,8,256]{2,1,0:T(8,128)(2,1)}, u32[]{:S(2)}) copy-start(bf16[4,8,256]{2,1,0:T(8,128)(2,1)} %param.30) | copy-start | bytes 49156
  192.7 18.4 %copy-start.29 = (f32[1,256]{1,0:T(1,128)S(1)}, f32[1,256]{1,0:T(1,128)}, u32[]{:S(2)}) copy-start(f32[1,256]{1,0:T(1,128)} %copy-done.28) | copy-start | bytes 3076
  192.7 18.4 %copy-start.31 = (f32[1,256]{1,0:T(1,128)S(1)}, f32[1,256]{1,0:T(1,128)}, u32[]{:S(2)}) copy-start(f32[1,256]{1,0:T(1,128)} %copy-done.30) | copy-start | bytes 3076
  192.7 18.4 %copy-start.33 = (f32[1,256]{1,0:T(1,128)S(1)}, f32[1,256]{1,0:T(1,128)}, u32[]{:S(2)}) copy-start(f32[1,256]{1,0:T(1,128)} %copy-done.32) | copy-start | bytes 3076
  192.7 18.4 %copy-start.35 = (f32[1,256]{1,0:T(1,128)S(1)}, f32[1,256]{1,0:T(1,128)}, u32[]{:S(2)}) copy-start(f32[1,256]{1,0:T(1,128)} %copy-done.34) | copy-start | bytes 3076
  192.8 2.3 collective-permute-start.17
  193.7 18.5 %collective-permute-start.25 = (bf16[3,1,2048]{0,2,1:T(8,128)(2,1)S(1)}, bf16[3,1,2048]{0,2,1:T(8,128)(2,1)S(1)}, u32[]{:S(2)}, u32[]{:S(2)}) collective-permute-start(bf16[3,1,2048]{0,2,1:T(8,128)(2,1)S(1)} %copy-done.8), channel_id=1, source_target_pairs={{0,4},{4,0},{8,12},{12,8},{16,20},{20,16},{24,28},{28,24},{32,36},... | collective-permute-start | bytes 36872 | tf_op jit(solution)/shard_map/ppermute | solution.py:21
  195.0 48.9 %copy-start.38 = (f32[8]{0:T(128)}, f32[8]{0:T(128)S(1)}, u32[]{:S(2)}) copy-start(f32[8]{0:T(128)S(1)} %get-tuple-element.61) | copy-start | bytes 100
  195.7 3.6 %collective-permute-start.18 = (bf16[3,1,256]{2,0,1:T(4,128)(2,1)S(1)}, bf16[3,1,256]{2,0,1:T(4,128)(2,1)S(1)}, u32[]{:S(2)}, u32[]{:S(2)}) collective-permute-start(bf16[3,1,256]{2,0,1:T(4,128)(2,1)S(1)} %broadcast_select_fusion.3), channel_id=1, source_target_pairs={{0,24},{4,28},{8,0},{12,4},{16,8},{20,12},{24,16},{28,20},{32,56},... | collective-permute-start | bytes 4616 | tf_op jit(solution)/shard_map/ppermute | solution.py:21
  197.5 5.1 %collective-permute-start.19 = (bf16[3,1,256]{2,0,1:T(4,128)(2,1)S(1)}, bf16[3,1,256]{2,0,1:T(4,128)(2,1)S(1)}, u32[]{:S(2)}, u32[]{:S(2)}) collective-permute-start(bf16[3,1,256]{2,0,1:T(4,128)(2,1)S(1)} %broadcast_select_fusion.3), channel_id=1, source_target_pairs={{0,16},{4,20},{8,24},{12,28},{16,0},{20,4},{24,8},{28,12},{32,48},... | collective-permute-start | bytes 4616 | tf_op jit(solution)/shard_map/ppermute | solution.py:21
  197.5 5.1 %collective-permute-start.20 = (bf16[3,1,256]{2,0,1:T(4,128)(2,1)S(1)}, bf16[3,1,256]{2,0,1:T(4,128)(2,1)S(1)}, u32[]{:S(2)}, u32[]{:S(2)}) collective-permute-start(bf16[3,1,256]{2,0,1:T(4,128)(2,1)S(1)} %broadcast_select_fusion.3), channel_id=1, source_target_pairs={{0,8},{4,12},{8,16},{12,20},{16,24},{20,28},{24,0},{28,4},{32,40},... | collective-permute-start | bytes 4616 | tf_op jit(solution)/shard_map/ppermute | solution.py:21
  202.6 5.3 %collective-permute-start.21 = (bf16[3,1,256]{2,0,1:T(4,128)(2,1)S(1)}, bf16[3,1,256]{2,0,1:T(4,128)(2,1)S(1)}, u32[]{:S(2)}, u32[]{:S(2)}) collective-permute-start(bf16[3,1,256]{2,0,1:T(4,128)(2,1)S(1)} %select_select_fusion.1), channel_id=1, source_target_pairs={{0,96},{4,100},{8,104},{12,108},{16,112},{20,116},{24,120},{28,124... | collective-permute-start | bytes 4616 | tf_op jit(solution)/shard_map/ppermute | solution.py:21
  206.0 5.1 %collective-permute-start.22 = (bf16[3,1,256]{2,0,1:T(4,128)(2,1)S(1)}, bf16[3,1,256]{2,0,1:T(4,128)(2,1)S(1)}, u32[]{:S(2)}, u32[]{:S(2)}) collective-permute-start(bf16[3,1,256]{2,0,1:T(4,128)(2,1)S(1)} %select_select_fusion.1), channel_id=1, source_target_pairs={{0,64},{4,68},{8,72},{12,76},{16,80},{20,84},{24,88},{28,92},{32,9... | collective-permute-start | bytes 4616 | tf_op jit(solution)/shard_map/ppermute | solution.py:21
  206.0 5.1 %collective-permute-start.23 = (bf16[3,1,256]{2,0,1:T(4,128)(2,1)S(1)}, bf16[3,1,256]{2,0,1:T(4,128)(2,1)S(1)}, u32[]{:S(2)}, u32[]{:S(2)}) collective-permute-start(bf16[3,1,256]{2,0,1:T(4,128)(2,1)S(1)} %select_select_fusion.1), channel_id=1, source_target_pairs={{0,32},{4,36},{8,40},{12,44},{16,48},{20,52},{24,56},{28,60},{32,6... | collective-permute-start | bytes 4616 | tf_op jit(solution)/shard_map/ppermute | solution.py:21
  212.4 14.9 %collective-permute-start.26 = (bf16[3,1,2048]{0,2,1:T(8,128)(2,1)S(1)}, bf16[3,1,2048]{0,2,1:T(8,128)(2,1)S(1)}, u32[]{:S(2)}, u32[]{:S(2)}) collective-permute-start(bf16[3,1,2048]{0,2,1:T(8,128)(2,1)S(1)} %broadcast_select_fusion), channel_id=1, source_target_pairs={{0,24},{4,28},{8,0},{12,4},{16,8},{20,12},{24,16},{28,20},{32,56},... | collective-permute-start | bytes 36872 | tf_op jit(solution)/shard_map/ppermute | solution.py:21
  214.3 16.3 %collective-permute-start.27 = (bf16[3,1,2048]{0,2,1:T(8,128)(2,1)S(1)}, bf16[3,1,2048]{0,2,1:T(8,128)(2,1)S(1)}, u32[]{:S(2)}, u32[]{:S(2)}) collective-permute-start(bf16[3,1,2048]{0,2,1:T(8,128)(2,1)S(1)} %broadcast_select_fusion), channel_id=1, source_target_pairs={{0,16},{4,20},{8,24},{12,28},{16,0},{20,4},{24,8},{28,12},{32,48},... | collective-permute-start | bytes 36872 | tf_op jit(solution)/shard_map/ppermute | solution.py:21
  215.2 22.8 %collective-permute-start.28 = (bf16[3,1,2048]{0,2,1:T(8,128)(2,1)S(1)}, bf16[3,1,2048]{0,2,1:T(8,128)(2,1)S(1)}, u32[]{:S(2)}, u32[]{:S(2)}) collective-permute-start(bf16[3,1,2048]{0,2,1:T(8,128)(2,1)S(1)} %broadcast_select_fusion), channel_id=1, source_target_pairs={{0,8},{4,12},{8,16},{12,20},{16,24},{20,28},{24,0},{28,4},{32,40},... | collective-permute-start | bytes 36872 | tf_op jit(solution)/shard_map/ppermute | solution.py:21
  238.1 14.9 %collective-permute-start.29 = (bf16[3,1,2048]{0,2,1:T(8,128)(2,1)S(1)}, bf16[3,1,2048]{0,2,1:T(8,128)(2,1)S(1)}, u32[]{:S(2)}, u32[]{:S(2)}) collective-permute-start(bf16[3,1,2048]{0,2,1:T(8,128)(2,1)S(1)} %select_select_fusion), channel_id=1, source_target_pairs={{0,96},{4,100},{8,104},{12,108},{16,112},{20,116},{24,120},{28,124... | collective-permute-start | bytes 36872 | tf_op jit(solution)/shard_map/ppermute | solution.py:21
  239.0 16.3 %collective-permute-start.30 = (bf16[3,1,2048]{0,2,1:T(8,128)(2,1)S(1)}, bf16[3,1,2048]{0,2,1:T(8,128)(2,1)S(1)}, u32[]{:S(2)}, u32[]{:S(2)}) collective-permute-start(bf16[3,1,2048]{0,2,1:T(8,128)(2,1)S(1)} %select_select_fusion), channel_id=1, source_target_pairs={{0,64},{4,68},{8,72},{12,76},{16,80},{20,84},{24,88},{28,92},{32,9... | collective-permute-start | bytes 36872 | tf_op jit(solution)/shard_map/ppermute | solution.py:21
  240.3 25.2 %collective-permute-start.31 = (bf16[3,1,2048]{0,2,1:T(8,128)(2,1)S(1)}, bf16[3,1,2048]{0,2,1:T(8,128)(2,1)S(1)}, u32[]{:S(2)}, u32[]{:S(2)}) collective-permute-start(bf16[3,1,2048]{0,2,1:T(8,128)(2,1)S(1)} %select_select_fusion), channel_id=1, source_target_pairs={{0,32},{4,36},{8,40},{12,44},{16,48},{20,52},{24,56},{28,60},{32,6... | collective-permute-start | bytes 36872 | tf_op jit(solution)/shard_map/ppermute | solution.py:21
  269.6 3.1 %collective-permute-start.24 = (f32[1,32,64,64]{3,2,1,0:T(8,128)S(1)}, f32[1,32,64,64]{3,2,1,0:T(8,128)}, u32[]{:S(2)}, u32[]{:S(2)}) collective-permute-start(f32[1,32,64,64]{3,2,1,0:T(8,128)S(1)} %add_select_fusion), channel_id=1, source_target_pairs={{0,4},{4,0},{8,12},{12,8},{16,20},{20,16},{24,28},{28,24},{32,36},... | collective-permute-start | bytes 1572872 | tf_op jit(solution)/shard_map/ppermute | solution.py:21
  (39 other events, 242.0 us)
Sparse Core Ops, SparseCore 0:
  192.9 78.4 reduce-scatter.1
